TPU v7x, 256 devices: a whole 4x4x8 slice. The times are simulated.
256 devices in a mesh: row: 4 (over y), col: 64 (over z, x, core).
Axes of the slice: x: 4, y: 4, z: 8, core: 2. Of those that a mesh axis runs over, the one named last changes fastest.
Arguments:
- tokens: bfloat16 [32768, 4096], P(('row', 'col')), may hold values from -6 to 6
- expert_ids: int32 [32768, 2], P(('row', 'col')), may hold values from 0 to 63, all different within a row; in each aligned block of 128 rows (0 to 127, 128 to 255, ...) at most 5 rows name the same one
- gate_weights: float32 [32768, 2], P(('row', 'col')), may hold values from 0.1 to 1
- w_gate: bfloat16 [64, 4096, 1536], P('col', None, 'row'), may hold values from -0.09375 to 0.09375
- w_up: bfloat16 [64, 4096, 1536], P('col', None, 'row'), may hold values from -0.09375 to 0.09375
- w_down: bfloat16 [64, 1536, 4096], P('col', None, 'row'), may hold values from -0.15625 to 0.15625
Outputs:
- moe_out: bfloat16 [32768, 4096], P(('row', 'col'))
Inputs may be any that keep to these rules, and one draw needn't show every extreme that they name: `expert_ids`: each row names 2 different experts. Among the 128 rows of one device no expert is named by more than 5 rows, and in every draw some expert is named by exactly 5 rows of some device.
All inputs are finite; a program needn't handle non-finite values.
Results may differ from a plain program's by a relative error of at most 0.0058.
Values may be sent and summed in bfloat16 or wider, within the bound.
No kernel may reach another device: no remote copies, remote signals or barrier semaphores. Data moves between devices by JAX's collectives and lax.ppermute only.
A program may use at most 128 MiB of HBM per device.

v0:
```python
import jax
import jax.numpy as jnp
from jax import lax
from jax.sharding import PartitionSpec as P


def local(tokens, expert_ids, gate_weights, w_gate, w_up, w_down):
    token_count, top_count = expert_ids.shape
    width = tokens.shape[1]
    local_count = w_gate.shape[0]
    unit_count = w_gate.shape[2]
    quarter = w_down.shape[2]
    columns = lax.axis_size("col")
    groups = lax.axis_size("row")
    experts = local_count * columns
    capacity = max(2, token_count * top_count * 5 // (4 * experts))
    flat_ids = expert_ids.reshape(-1)
    onehot = (flat_ids[:, None] == jnp.arange(experts, dtype=jnp.int32)[None, :]).astype(jnp.int32)
    earlier = jnp.cumsum(onehot, axis=0) - onehot
    position = jnp.sum(earlier * onehot, axis=1)
    slot_ids = (flat_ids * capacity + position).reshape(token_count, top_count)
    chooser = jnp.any(
        jnp.arange(experts * capacity, dtype=jnp.int32)[:, None, None] == slot_ids[None, :, :],
        axis=2,
    ).astype(jnp.bfloat16)
    outgoing = jnp.dot(chooser, tokens, preferred_element_type=jnp.float32).astype(jnp.bfloat16)
    outgoing = outgoing.reshape(columns, local_count * capacity, width)
    arrived = lax.all_to_all(outgoing, "col", split_axis=0, concat_axis=0, tiled=True)
    block_rows = lax.all_gather(arrived[None], "row", axis=0, tiled=True)
    count = block_rows.shape[0]
    grouped = block_rows.reshape(count, columns, local_count, capacity, width)
    expert = 0
    inputs = grouped[:, :, expert].reshape(-1, width)
    gate_part = jnp.dot(inputs, w_gate[expert], preferred_element_type=jnp.float32)
    up_part = jnp.dot(inputs, w_up[expert], preferred_element_type=jnp.float32)
    hidden = (jax.nn.silu(gate_part) * up_part).astype(jnp.bfloat16)
    outputs = hidden.reshape(count, columns, 1, capacity, unit_count)
    hidden_all = outputs.reshape(count, columns, local_count * capacity, unit_count)
    hidden_split = hidden_all.reshape(groups, columns, local_count, capacity, unit_count)
    piece = lax.all_gather(hidden_split, "row", axis=4, tiled=True)
    count = piece.shape[4]
    expert = 0
    rows = piece[:, :, expert].reshape(-1, count)
    block = w_down[expert]
    parts = [jnp.dot(rows, block, preferred_element_type=jnp.float32)]
    summed = jnp.stack(parts)
    expert_out = summed.astype(jnp.bfloat16).reshape(
        local_count, groups, columns, capacity, quarter
    )
    expert_out = jnp.transpose(expert_out, (1, 2, 0, 3, 4)).reshape(
        groups, columns, local_count * capacity, quarter
    )
    colwise = lax.all_to_all(expert_out, "col", split_axis=1, concat_axis=1, tiled=True)
    home = lax.all_to_all(colwise, "row", split_axis=0, concat_axis=3, tiled=True)
    results = home.reshape(experts * capacity, width)
    shares = gate_weights / jnp.sum(gate_weights, axis=1, keepdims=True)
    picked = results[slot_ids].astype(jnp.float32)
    combined = jnp.sum(shares[:, :, None] * picked, axis=1)
    return combined.astype(jnp.bfloat16)


def solution(mesh):
    placed = (
        P(("row", "col"), None),
        P(("row", "col"), None),
        P(("row", "col"), None),
        P("col", None, "row"),
        P("col", None, "row"),
        P("col", None, "row"),
    )
    return jax.shard_map(
        local, mesh=mesh, in_specs=placed, out_specs=P(("row", "col"), None), check_vma=False
    )
```

profile of v0, /device:TPU:1, one launch (start us, length us, event | category | flops | bytes accessed | tf_op | source)
XLA Modules:
  0.0 528.3 jit_solution(9375818899468450079)
XLA Ops:
  6.5 0.9 copy.41
  7.6 0.1 eq.39
  7.8 0.6 reduce-window.6
  8.4 0.2 slice_reduce_fusion
  8.7 0.1 reduce_sum.31
  8.9 0.7 compare_select_fusion
  9.7 3.6 convolution_convert_fusion
  13.3 4.7 reshape.38
  18.0 107.6 %all_to_all.25 = bf16[64,5,4096]{2,1,0:T(8,128)(2,1)S(1)} all-to-all(bf16[64,5,4096]{2,1,0:T(8,128)(2,1)} %reshape.38), channel_id=1, replica_groups=mesh['row'=4,'col'=64] {'col'}, dimensions={0} | all-to-all | bytes 5242880 | tf_op jit(solution)/shard_map/all_to_all | solution.py:28
  125.6 3.2 copy.45
  128.8 0.3 all-gather.4.cloned.1.call-start
  129.2 101.0 %all-gather.6.cloned.1.call-done = bf16[256,5,4096]{2,0,1:T(8,128)(2,1)} async-done(((bf16[64,5,4096]{2,0,1:T(8,128)(2,1)}), bf16[256,5,4096]{2,0,1:T(8,128)(2,1)}) %all-gather.6.cloned.1.call-update) | async-done | bytes 10485776 | tf_op jit(solution)/shard_map/all_gather | solution.py:29
  230.2 15.2 %copy.46 = bf16[256,5,4096]{2,1,0:T(8,128)(2,1)} copy(bf16[256,5,4096]{2,0,1:T(8,128)(2,1)} %all-gather.6.cloned.1.call-done) | data formatting | bytes 20971520 | tf_op jit(solution)/shard_map/all_gather | solution.py:29
  245.4 16.8 %reshape_squeeze_reshape.3 = bf16[1280,4096]{1,0:T(8,128)(2,1)} reshape(bf16[256,5,4096]{2,1,0:T(8,128)(2,1)} %copy.46) | data formatting | bytes 20971520 | tf_op jit(solution)/shard_map/reshape;squeeze;reshape | solution.py:33
  262.3 9.3 %fusion.2 = f32[1280,384]{1,0:T(8,128)S(1)} fusion(bf16[1280,4096]{1,0:T(8,128)(2,1)} %reshape_squeeze_reshape.3, bf16[1,4096,384]{2,1,0:T(8,128)(2,1)} %param.9), kind=kOutput, calls=%fused_computation.7 | convolution fusion | flops 4026531840 | bytes 15597568 | tf_op jit(solution)/shard_map/dot_general | solution.py:34
  271.6 6.9 %fusion.4 = bf16[1280,384]{1,0:T(8,128)(2,1)} fusion(bf16[1280,4096]{1,0:T(8,128)(2,1)S(1)} %copy-done.1, bf16[1,4096,384]{2,1,0:T(8,128)(2,1)S(1)} %copy-done.3, f32[1280,384]{1,0:T(8,128)S(1)} %fusion.2), kind=kOutput, calls=%fused_computation.9 | convolution fusion | flops 4029480960 | bytes 16580608 | tf_op jit(solution)/shard_map/dot_general | solution.py:35
  278.6 3.0 reshape_reshape_reshape.3
  281.5 69.4 %all-gather.4.cloned.1.call-done = bf16[4,64,1,5,1536]{4,3,1,0,2:T(8,128)(2,1)} async-done(((bf16[4,64,1,5,384]{4,3,1,0,2:T(8,128)(2,1)}), bf16[4,64,1,5,1536]{4,3,1,0,2:T(8,128)(2,1)}) %all-gather.4.cloned.1.call-update) | async-done | bytes 3932176 | tf_op jit(solution)/shard_map/all_gather | solution.py:40
  351.0 7.6 %reshape_squeeze.3 = bf16[1280,1536]{1,0:T(8,128)(2,1)} reshape(bf16[4,64,1,5,1536]{4,3,1,0,2:T(8,128)(2,1)} %all-gather.4.cloned.1.call-done) | data formatting | bytes 7864320 | tf_op jit(solution)/shard_map/reshape;squeeze | solution.py:43
  358.6 7.6 %convolution_convert_fusion.1 = bf16[1280,1024]{1,0:T(8,128)(2,1)} fusion(bf16[1280,1536]{1,0:T(8,128)(2,1)} %reshape_squeeze.3, bf16[1,1536,1024]{2,1,0:T(8,128)(2,1)S(1)} %copy-done), kind=kOutput, calls=%fused_computation.3 | convolution fusion | flops 4027842560 | bytes 9699328 | tf_op jit(solution)/shard_map/dot_general | solution.py:45
  366.2 6.5 %reshape_transpose_reshape.3 = bf16[4,64,5,1024]{3,2,1,0:T(8,128)(2,1)} reshape(bf16[1280,1024]{1,0:T(8,128)(2,1)} %convolution_convert_fusion.1) | data formatting | bytes 5242880 | tf_op jit(solution)/shard_map/reshape;transpose;reshape | solution.py:50
  372.8 7.3 %copy.47 = bf16[4,64,5,1024]{3,0,2,1:T(4,128)(2,1)S(1)} copy(bf16[4,64,5,1024]{3,2,1,0:T(8,128)(2,1)} %reshape_transpose_reshape.3) | data formatting | bytes 5242880 | tf_op jit(solution)/shard_map/reshape;transpose;reshape | solution.py:50
  380.1 73.2 %all_to_all.26 = bf16[4,64,5,1024]{3,0,2,1:T(4,128)(2,1)S(1)} all-to-all(bf16[4,64,5,1024]{3,0,2,1:T(4,128)(2,1)S(1)} %copy.47), channel_id=1, replica_groups=mesh['row'=4,'col'=64] {'col'}, dimensions={1} | all-to-all | bytes 5242880 | tf_op jit(solution)/shard_map/all_to_all | solution.py:53
  453.3 2.3 copy.48
  455.7 4.8 all-to-all-start.2
  460.6 0.1 reshape.42
  460.9 31.4 %all-to-all-done.2 = bf16[4,64,5,1024]{3,1,2,0:T(8,128)(2,1)} async-done(((bf16[4,64,5,1024]{3,1,2,0:T(8,128)(2,1)}), bf16[4,64,5,1024]{3,1,2,0:T(8,128)(2,1)}, u32[]{:S(2)}, u32[]{:S(2)}) %all-to-all-start.2) | async-done | bytes 2621472 | tf_op jit(solution)/shard_map/all_to_all | solution.py:54
  492.3 3.8 copy.49
  496.0 2.6 copy.52
  498.7 7.3 %gather_fusion = bf16[256,4096]{1,0:T(8,128)(2,1)} fusion(bf16[320,4096]{1,0:T(8,128)(2,1)} %bitcast.43, s32[1024]{0:T(1024)S(1)} %pad_clamp_fusion), kind=kCustom, calls=%fused_computation | custom fusion | bytes 4195328 | tf_op jit(solution)/shard_map/gather | solution.py:57
  506.0 5.6 %reshape.52 = f32[128,2,4096]{2,1,0:T(2,128)} reshape(bf16[256,4096]{1,0:T(8,128)(2,1)} %gather_fusion) | data formatting | bytes 6291456 | tf_op jit(solution)/shard_map/convert_element_type | solution.py:57
  511.6 9.6 %multiply_reduce_fusion = bf16[128,4096]{1,0:T(8,128)(2,1)} fusion(f32[128,2,4096]{2,1,0:T(2,128)} %reshape.52, f32[128,2]{1,0:T(8,128)S(1)} %copy.40), kind=kLoop, calls=%fused_computation.2 | loop fusion | flops 1572864 | bytes 5243904 | tf_op jit(solution)/shard_map/reduce_sum | solution.py:58
  (23 shorter events, 0.7 us)
Async XLA Ops:
  6.5 352.1 %copy-start = (bf16[1,1536,1024]{2,1,0:T(8,128)(2,1)S(1)}, bf16[1,1536,1024]{2,1,0:T(8,128)(2,1)}, u32[]{:S(2)}) copy-start(bf16[1,1536,1024]{2,1,0:T(8,128)(2,1)} %param.11) | copy-start | bytes 9437188
  6.5 223.7 %all-gather.6.cloned.1.call-start = ((), (), s32[]{:S(2)}) async-start(), calls=%async_computation.4 | async-start | bytes 13107200 | tf_op jit(solution)/shard_map/all_gather | solution.py:29
  128.8 222.1 %all-gather.4.cloned.1.call-start = ((), (), s32[]{:S(2)}) async-start(), calls=%async_computation.3 | async-start | bytes 7864320 | tf_op jit(solution)/shard_map/all_gather | solution.py:40
  262.3 9.4 %copy-start.1 = (bf16[1280,4096]{1,0:T(8,128)(2,1)S(1)}, bf16[1280,4096]{1,0:T(8,128)(2,1)}, u32[]{:S(2)}) copy-start(bf16[1280,4096]{1,0:T(8,128)(2,1)} %reshape_squeeze_reshape.3) | copy-start | bytes 31457284
  262.3 9.4 %copy-start.3 = (bf16[1,4096,384]{2,1,0:T(8,128)(2,1)S(1)}, bf16[1,4096,384]{2,1,0:T(8,128)(2,1)}, u32[]{:S(2)}) copy-start(bf16[1,4096,384]{2,1,0:T(8,128)(2,1)} %param.10) | copy-start | bytes 9437188
  455.6 5.1 copy-start.2
  455.7 36.6 %all-to-all-start.2 = ((bf16[4,64,5,1024]{3,1,2,0:T(8,128)(2,1)}), bf16[4,64,5,1024]{3,1,2,0:T(8,128)(2,1)}, u32[]{:S(2)}, u32[]{:S(2)}) async-start(bf16[4,64,5,1024]{3,1,2,0:T(8,128)(2,1)} %copy.48), calls=%async_computation.2 | async-start | bytes 5242880 | tf_op jit(solution)/shard_map/all_to_all | solution.py:54
Sparse Core Ops, SparseCore 0:
  128.9 101.2 all-gather.5
  281.7 69.2 all-gather.3
where the time goes:
time: 534 us; the launch traced here: 528 us
  waiting for transfers between devices  202 us (38%)
  blocking collectives  181 us (34%)
  local copies, waits for them, and re-layouts  88.1 us (16%)
  matrix products  27.4 us (5%)
  between operations  13.7 us (3%)
  other arithmetic  11.2 us (2%)
    all_to_all x1, blocking collectives, local(): lax.all_to_all(outgoing, 'col', split_axis=0, concat_axis=0, tiled=True)  108 us
    all_gather x1, waiting for transfers between devices, local(): block_rows = lax.all_gather(arrived[None], 'row', axis=0, tiled=True)  101 us
    all_to_all x1, blocking collectives, local(): lax.all_to_all(expert_out, 'col', split_axis=1, concat_axis=1, tiled=True)  73.2 us
    all_gather x1, waiting for transfers between devices, local(): piece = lax.all_gather(hidden_split, 'row', axis=4, tiled=True)  69.4 us
    all_to_all x1, waiting for transfers between devices, local(): lax.all_to_all(colwise, 'row', split_axis=0, concat_axis=3, tiled=True)  31.4 us
    another operation x1, local copies, waits for them, and re-layouts, local(): inputs = grouped[:, :, expert].reshape(-1, width)  16.8 us
    all_gather x1, local copies, waits for them, and re-layouts, local(): block_rows = lax.all_gather(arrived[None], 'row', axis=0, tiled=True)  15.2 us
    another operation x2, local copies, waits for them, and re-layouts, local(): jnp.transpose(expert_out, (1, 2, 0, 3, 4))  13.9 us
  transfers between devices with their start and end apart: 3, of which 3 were waited for; matrix products, arithmetic and copies ran while one was open for 0% of the time, Pallas kernels for 0%

commit v1 on v0

--- a/solution.py
+++ b/solution.py
@@ -50,7 +50,12 @@
     expert_out = jnp.transpose(expert_out, (1, 2, 0, 3, 4)).reshape(
         groups, columns, local_count * capacity, quarter
     )
-    colwise = lax.all_to_all(expert_out, "col", split_axis=1, concat_axis=1, tiled=True)
+    colwise = jnp.concatenate(
+        lax.all_to_all(
+            jnp.stack(jnp.split(expert_out, lax.axis_size("col"), axis=1), axis=0), "col", 0, 0
+        ),
+        axis=1,
+    )
     home = lax.all_to_all(colwise, "row", split_axis=0, concat_axis=3, tiled=True)
     results = home.reshape(experts * capacity, width)
     shares = gate_weights / jnp.sum(gate_weights, axis=1, keepdims=True)

time: 534 us -> 588 us (1.10)
  local copies, waits for them, and re-layouts: 88.1 us -> 140 us
    unnamed x10 -> x73, local copies, waits for them, and re-layouts: 3.59 us -> 56.7 us
    another operation x2 -> x1, local copies, waits for them, and re-layouts: 13.9 us -> 6.54 us  [local(): jnp.transpose(expert_out, (1, 2, 0, 3, 4))]
    another operation x1 -> x3, local copies, waits for them, and re-layouts: 0.01 us -> 6 us  [the longest x2 6 us: local(): jnp.stack(jnp.split(expert_out, lax.axis_size('col'), axis=1), axis=0)]
where the time goes in v1:
time: 588 us; the launch traced here: 580 us
  waiting for transfers between devices  202 us (34%)
  blocking collectives  181 us (31%)
  local copies, waits for them, and re-layouts  140 us (24%)
  matrix products  27.4 us (5%)
  between operations  13.8 us (2%)
  other arithmetic  11.2 us (2%)
    all_to_all x1, blocking collectives, local(): lax.all_to_all(outgoing, 'col', split_axis=0, concat_axis=0, tiled=True)  108 us
    all_gather x1, waiting for transfers between devices, local(): block_rows = lax.all_gather(arrived[None], 'row', axis=0, tiled=True)  101 us
    all_to_all x1, blocking collectives, local(): lax.all_to_all(jnp.stack(jnp.split(expert_out, lax.axis_size('col'), axis...  73.2 us
    all_gather x1, waiting for transfers between devices, local(): piece = lax.all_gather(hidden_split, 'row', axis=4, tiled=True)  69.4 us
    unnamed x73, local copies, waits for them, and re-layouts  56.7 us
    all_to_all x1, waiting for transfers between devices, local(): lax.all_to_all(colwise, 'row', split_axis=0, concat_axis=3, tiled=True)  31.4 us
    another operation x1, local copies, waits for them, and re-layouts, local(): inputs = grouped[:, :, expert].reshape(-1, width)  16.8 us
    all_gather x1, local copies, waits for them, and re-layouts, local(): block_rows = lax.all_gather(arrived[None], 'row', axis=0, tiled=True)  15.2 us
  transfers between devices with their start and end apart: 3, of which 3 were waited for; matrix products, arithmetic and copies ran while one was open for 0% of the time, Pallas kernels for 0%

profile of v1, /device:TPU:1, one launch (start us, length us, event | category | flops | bytes accessed | tf_op | source)
XLA Modules:
  0.0 580.0 jit_solution(10471791807503010292)
XLA Ops:
  6.5 0.9 copy.293
  9.7 3.6 convolution_convert_fusion
  13.3 4.7 reshape.44
  18.0 107.6 %all_to_all.25 = bf16[64,5,4096]{2,1,0:T(8,128)(2,1)S(1)} all-to-all(bf16[64,5,4096]{2,1,0:T(8,128)(2,1)} %reshape.44), channel_id=1, replica_groups=mesh['row'=4,'col'=64] {'col'}, dimensions={0} | all-to-all | bytes 5242880 | tf_op jit(solution)/shard_map/all_to_all | solution.py:28
  125.6 3.2 copy.297
  129.2 101.0 %all-gather.6.cloned.1.call-done = bf16[256,5,4096]{2,0,1:T(8,128)(2,1)} async-done(((bf16[64,5,4096]{2,0,1:T(8,128)(2,1)}), bf16[256,5,4096]{2,0,1:T(8,128)(2,1)}) %all-gather.6.cloned.1.call-update) | async-done | bytes 10485776 | tf_op jit(solution)/shard_map/all_gather | solution.py:29
  230.2 15.2 %copy.298 = bf16[256,5,4096]{2,1,0:T(8,128)(2,1)} copy(bf16[256,5,4096]{2,0,1:T(8,128)(2,1)} %all-gather.6.cloned.1.call-done) | data formatting | bytes 20971520 | tf_op jit(solution)/shard_map/all_gather | solution.py:29
  245.4 16.8 %reshape_squeeze_reshape.3 = bf16[1280,4096]{1,0:T(8,128)(2,1)} reshape(bf16[256,5,4096]{2,1,0:T(8,128)(2,1)} %copy.298) | data formatting | bytes 20971520 | tf_op jit(solution)/shard_map/reshape;squeeze;reshape | solution.py:33
  262.3 9.3 %fusion.2 = f32[1280,384]{1,0:T(8,128)S(1)} fusion(bf16[1280,4096]{1,0:T(8,128)(2,1)} %reshape_squeeze_reshape.3, bf16[1,4096,384]{2,1,0:T(8,128)(2,1)} %param.9), kind=kOutput, calls=%fused_computation.7 | convolution fusion | flops 4026531840 | bytes 15597568 | tf_op jit(solution)/shard_map/dot_general | solution.py:34
  271.6 6.9 %fusion.4 = bf16[1280,384]{1,0:T(8,128)(2,1)} fusion(bf16[1280,4096]{1,0:T(8,128)(2,1)S(1)} %copy-done.1, bf16[1,4096,384]{2,1,0:T(8,128)(2,1)S(1)} %copy-done.3, f32[1280,384]{1,0:T(8,128)S(1)} %fusion.2), kind=kOutput, calls=%fused_computation.9 | convolution fusion | flops 4029480960 | bytes 16580608 | tf_op jit(solution)/shard_map/dot_general | solution.py:35
  278.6 3.0 reshape_reshape_reshape.3
  281.5 69.4 %all-gather.4.cloned.1.call-done = bf16[4,64,1,5,1536]{4,3,1,0,2:T(8,128)(2,1)} async-done(((bf16[4,64,1,5,384]{4,3,1,0,2:T(8,128)(2,1)}), bf16[4,64,1,5,1536]{4,3,1,0,2:T(8,128)(2,1)}) %all-gather.4.cloned.1.call-update) | async-done | bytes 3932176 | tf_op jit(solution)/shard_map/all_gather | solution.py:40
  351.0 7.6 %reshape_squeeze.3 = bf16[1280,1536]{1,0:T(8,128)(2,1)} reshape(bf16[4,64,1,5,1536]{4,3,1,0,2:T(8,128)(2,1)} %all-gather.4.cloned.1.call-done) | data formatting | bytes 7864320 | tf_op jit(solution)/shard_map/reshape;squeeze | solution.py:43
  358.6 7.6 %convolution_convert_fusion.1 = bf16[1280,1024]{1,0:T(8,128)(2,1)} fusion(bf16[1280,1536]{1,0:T(8,128)(2,1)} %reshape_squeeze.3, bf16[1,1536,1024]{2,1,0:T(8,128)(2,1)S(1)} %copy-done), kind=kOutput, calls=%fused_computation.3 | convolution fusion | flops 4027842560 | bytes 9699328 | tf_op jit(solution)/shard_map/dot_general | solution.py:45
  366.2 6.5 %reshape_transpose_reshape.3 = bf16[4,64,5,1024]{3,2,1,0:T(8,128)(2,1)} reshape(bf16[1280,1024]{1,0:T(8,128)(2,1)} %convolution_convert_fusion.1) | data formatting | bytes 5242880 | tf_op jit(solution)/shard_map/reshape;transpose;reshape | solution.py:50
  372.8 0.8 constant_dynamic-update-slice_fusion.63
  374.5 0.8 constant_dynamic-update-slice_fusion.61
  385.4 0.8 constant_dynamic-update-slice_fusion.48
  387.1 0.8 constant_dynamic-update-slice_fusion.46
  388.8 0.8 constant_dynamic-update-slice_fusion.44
  390.5 0.8 constant_dynamic-update-slice_fusion.42
  401.5 0.8 constant_dynamic-update-slice_fusion.29
  426.8 5.2 copy.362
  431.9 73.2 %all_to_all.26 = bf16[64,4,1,5,1024]{4,1,3,2,0:T(4,128)(2,1)S(1)} all-to-all(bf16[64,4,1,5,1024]{4,1,3,2,0:T(4,128)(2,1)S(1)} %copy.362), channel_id=1, replica_groups=mesh['row'=4,'col'=64] {'col'}, dimensions={0} | all-to-all | bytes 5242880 | tf_op jit(solution)/shard_map/all_to_all | solution.py:54
  505.2 2.3 copy.363
  507.5 4.7 all-to-all-start.2
  512.6 31.4 %all-to-all-done.2 = bf16[4,64,5,1024]{3,1,2,0:T(8,128)(2,1)} async-done(((bf16[4,64,5,1024]{3,1,2,0:T(8,128)(2,1)}), bf16[4,64,5,1024]{3,1,2,0:T(8,128)(2,1)}, u32[]{:S(2)}, u32[]{:S(2)}) %all-to-all-start.2) | async-done | bytes 2621472 | tf_op jit(solution)/shard_map/all_to_all | solution.py:59
  544.0 3.8 copy.364
  547.8 2.6 copy.430
  550.4 7.3 %gather_fusion = bf16[256,4096]{1,0:T(8,128)(2,1)} fusion(bf16[320,4096]{1,0:T(8,128)(2,1)} %bitcast.428, s32[1024]{0:T(1024)S(1)} %pad_clamp_fusion), kind=kCustom, calls=%fused_computation | custom fusion | bytes 4195328 | tf_op jit(solution)/shard_map/gather | solution.py:62
  557.7 5.6 reshape.60
  563.3 9.6 %multiply_reduce_fusion = bf16[128,4096]{1,0:T(8,128)(2,1)} fusion(f32[128,2,4096]{2,1,0:T(2,128)} %reshape.60, f32[128,2]{1,0:T(8,128)S(1)} %copy.292), kind=kLoop, calls=%fused_computation.2 | loop fusion | flops 1572864 | bytes 5243904 | tf_op jit(solution)/shard_map/reduce_sum | solution.py:63
  (87 shorter events, 51.0 us)
Async XLA Ops:
  6.5 352.1 %copy-start = (bf16[1,1536,1024]{2,1,0:T(8,128)(2,1)S(1)}, bf16[1,1536,1024]{2,1,0:T(8,128)(2,1)}, u32[]{:S(2)}) copy-start(bf16[1,1536,1024]{2,1,0:T(8,128)(2,1)} %param.11) | copy-start | bytes 9437188
  6.5 223.7 %all-gather.6.cloned.1.call-start = ((), (), s32[]{:S(2)}) async-start(), calls=%async_computation.4 | async-start | bytes 13107200 | tf_op jit(solution)/shard_map/all_gather | solution.py:29
  128.8 222.1 %all-gather.4.cloned.1.call-start = ((), (), s32[]{:S(2)}) async-start(), calls=%async_computation.3 | async-start | bytes 7864320 | tf_op jit(solution)/shard_map/all_gather | solution.py:40
  262.3 9.4 %copy-start.1 = (bf16[1280,4096]{1,0:T(8,128)(2,1)S(1)}, bf16[1280,4096]{1,0:T(8,128)(2,1)}, u32[]{:S(2)}) copy-start(bf16[1280,4096]{1,0:T(8,128)(2,1)} %reshape_squeeze_reshape.3) | copy-start | bytes 31457284
  262.3 9.4 %copy-start.3 = (bf16[1,4096,384]{2,1,0:T(8,128)(2,1)S(1)}, bf16[1,4096,384]{2,1,0:T(8,128)(2,1)}, u32[]{:S(2)}) copy-start(bf16[1,4096,384]{2,1,0:T(8,128)(2,1)} %param.10) | copy-start | bytes 9437188
  505.1 7.3 %copy-start.2 = (f32[128,2]{0,1:T(2,128)S(1)}, f32[128,2]{0,1:T(2,128)}, u32[]{:S(2)}) copy-start(f32[128,2]{0,1:T(2,128)} %param.8) | copy-start | bytes 3076
  507.5 36.5 %all-to-all-start.2 = ((bf16[4,64,5,1024]{3,1,2,0:T(8,128)(2,1)}), bf16[4,64,5,1024]{3,1,2,0:T(8,128)(2,1)}, u32[]{:S(2)}, u32[]{:S(2)}) async-start(bf16[4,64,5,1024]{3,1,2,0:T(8,128)(2,1)} %copy.363), calls=%async_computation.2 | async-start | bytes 5242880 | tf_op jit(solution)/shard_map/all_to_all | solution.py:59
Sparse Core Ops, SparseCore 0:
  128.9 101.2 all-gather.5
  281.7 69.2 all-gather.3
